TPU v7x, 512 devices: a whole 4x4x16 slice. The times are simulated.
512 devices in a mesh: gx: 32 (over z, core), gy: 16 (over x, y).
Axes of the slice: x: 4, y: 4, z: 16, core: 2. Of those that a mesh axis runs over, the one named last changes fastest.
Arguments:
- field: bfloat16 [1024, 65536], P('gx', 'gy'), may hold values from -6 to 6
- dw0: float32 [9, 32], replicated, may hold values from -2 to 2
- pw0: bfloat16 [32, 32], replicated, may hold values from -1.5 to 1.5
- dw1: float32 [9, 32], replicated, may hold values from -2 to 2
- pw1: bfloat16 [32, 64], replicated, may hold values from -1.5 to 1.5
- dw2: float32 [9, 64], replicated, may hold values from -2 to 2
- pw2: bfloat16 [64, 128], replicated, may hold values from -1 to 1
- dw3: float32 [9, 128], replicated, may hold values from -2 to 2
- pw3: bfloat16 [128, 256], replicated, may hold values from -0.75 to 0.75
- dw4: float32 [9, 256], replicated, may hold values from -2 to 2
- pw4: bfloat16 [256, 512], replicated, may hold values from -0.5 to 0.5
- dwc: float32 [4, 9, 512], replicated, may hold values from -2 to 2
- pwc: bfloat16 [4, 512, 512], replicated, may hold values from -0.375 to 0.375
Outputs:
- fine: bfloat16 [1024, 65536], P('gx', 'gy')
- coarse: bfloat16 [4, 4096], replicated
All inputs are finite; a program needn't handle non-finite values.
Results may differ from a plain program's by a relative error of at most 0.024.
Values may be sent and summed in bfloat16 or wider, within the bound.
No kernel may reach another device: no remote copies, remote signals or barrier semaphores. Data moves between devices by JAX's collectives and lax.ppermute only.
A program may use at most 64 MiB of HBM per device.

v0:
```python
import jax
import jax.numpy as jnp
from jax import lax
from jax.sharding import PartitionSpec as P

LC = 4


def shifted(value, axis, steps):
    count = lax.axis_size(axis)
    leading, last = (max(0, -steps), min(count, count - steps))
    return lax.ppermute(value, axis, [(source, source + steps) for source in range(leading, last)])


def padded_2(block, sides, width):
    for axis, dim in sides:
        count = lax.axis_size(axis)
        forward = [(i, i + 1) for i in range(count - 1)]
        backward = [(target, source) for source, target in forward]
        low = lax.ppermute(
            lax.slice_in_dim(block, block.shape[dim] - width, None, axis=dim), axis, forward
        )
        high = lax.ppermute(lax.slice_in_dim(block, 0, width, axis=dim), axis, backward)
        block = jnp.concatenate([low, block, high], axis=dim)
    return block


def gelu_tanh(value):
    return jax.nn.gelu(value, approximate=True)


def point_flat(spread, weight, rows, cols):
    chans = weight.shape[0]
    flat = spread.astype(jnp.bfloat16).reshape(rows * cols, chans)
    mixed = jnp.dot(flat, weight, preferred_element_type=jnp.float32)
    return gelu_tanh(mixed).reshape(rows, cols * weight.shape[1])


def down_level(field, taps, weight, split_rows, split_cols):
    chans = taps.shape[1]
    rows = field.shape[0]
    cols = field.shape[1] // chans
    half_rows = rows // 2
    half_cols = cols // 2
    if split_rows:
        upper = shifted(field[-1:], "gx", 1)
    else:
        upper = jnp.zeros((1, cols * chans), jnp.bfloat16)
    extended = jnp.concatenate([upper, field], axis=0)
    if split_cols:
        leftside = shifted(extended[:, -chans:], "gy", 1)
    else:
        leftside = jnp.zeros((rows + 1, chans), jnp.bfloat16)
    tiled = jnp.tile(taps, (1, half_cols))
    total = jnp.zeros((half_rows, half_cols * chans), jnp.float32)
    for first in range(3):
        slab = extended[first : first + rows : 2]
        left_slab = leftside[first : first + rows : 2]
        pairs = slab.reshape(half_rows, half_cols, 2 * chans)
        even_cells = pairs[:, :, :chans].reshape(half_rows, half_cols * chans)
        odd_cells = pairs[:, :, chans:].reshape(half_rows, half_cols * chans)
        before = jnp.concatenate([left_slab, odd_cells[:, :-chans]], axis=1)
        for second, piece in enumerate((before, even_cells, odd_cells)):
            total = total + piece.astype(jnp.float32) * tiled[3 * first + second]
    return point_flat(total, weight, half_rows, half_cols).astype(jnp.bfloat16)


def local(field, dw0, pw0, dw1, pw1, dw2, pw2, dw3, pw3, dw4, pw4, dwc, pwc):
    chans = dw0.shape[1]
    rows = field.shape[0]
    cols = field.shape[1] // chans
    grid = field.reshape(rows, cols, chans)
    padded = padded_2(grid, (("gx", 0), ("gy", 1)), 2)
    flat_pad = padded.reshape(rows + 4, (cols + 4) * chans)
    tiled = jnp.tile(dw0, (1, cols))
    total = jnp.zeros((rows, cols * chans), jnp.float32)
    for first in range(3):
        for second in range(3):
            piece = flat_pad[
                2 * first : 2 * first + rows, 2 * second * chans : 2 * second * chans + cols * chans
            ]
            total = total + piece.astype(jnp.float32) * tiled[3 * first + second]
    hidden = (field.astype(jnp.float32) + point_flat(total, pw0, rows, cols)).astype(jnp.bfloat16)
    fine = hidden
    for taps, weight in ((dw1, pw1), (dw2, pw2), (dw3, pw3), (dw4, pw4)):
        hidden = down_level(hidden, taps, weight, True, True)
    coarse_chans = dwc.shape[2]
    finished = 0
    for level in range(LC):
        if (
            finished == level
            and hidden.shape[0] % 2 == 0
            and (hidden.shape[1] // coarse_chans % 2 == 0)
        ):
            hidden = down_level(hidden, dwc[level], pwc[level], True, True)
            finished = level + 1
    hidden = lax.all_gather(hidden, "gx", axis=0, tiled=True)
    hidden = lax.all_gather(hidden, "gy", axis=1, tiled=True)
    for level in range(finished, LC):
        hidden = down_level(hidden, dwc[level], pwc[level], False, False)
    return (fine, hidden)


def solution(mesh):
    placed = (P("gx", "gy"), P(), P(), P(), P(), P(), P(), P(), P(), P(), P(), P(), P())
    return jax.shard_map(
        local, mesh=mesh, in_specs=placed, out_specs=(P("gx", "gy"), P()), check_vma=False
    )
```

profile of v0, /device:TPU:2, one launch (start us, length us, event | category | flops | bytes accessed | tf_op | source)
XLA Modules:
  0.0 278.6 jit_solution(14854291314269597330)
XLA Ops:
  28.4 3.5 %collective-permute-start.2 = (bf16[36,2,32]{1,2,0:T(8,128)(2,1)S(1)}, bf16[36,2,32]{1,2,0:T(8,128)(2,1)S(1)}, u32[]{:S(2)}, u32[]{:S(2)}) collective-permute-start(bf16[36,2,32]{1,2,0:T(8,128)(2,1)S(1)} %get-tuple-element.8), channel_id=1, source_target_pairs={{0,1},{1,2},{2,3},{3,4},{4,5},{5,6},{6,7},{7,8},{8,9},{9,10},{10,1... | collective-permute-start | bytes 13832 | tf_op jit(solution)/shard_map/ppermute | solution.py:20
  31.9 4.5 %collective-permute-start.3 = (bf16[36,2,32]{1,2,0:T(8,128)(2,1)S(1)}, bf16[36,2,32]{1,2,0:T(8,128)(2,1)S(1)}, u32[]{:S(2)}, u32[]{:S(2)}) collective-permute-start(bf16[36,2,32]{1,2,0:T(8,128)(2,1)S(1)} %get-tuple-element.9), channel_id=1, source_target_pairs={{1,0},{2,1},{3,2},{4,3},{5,4},{6,5},{7,6},{8,7},{9,8},{10,9},{11,1... | collective-permute-start | bytes 13832 | tf_op jit(solution)/shard_map/ppermute | solution.py:23
  48.0 4.1 %collective-permute-start.4 = (bf16[1,4096]{1,0:T(2,128)(2,1)S(1)}, bf16[1,4096]{1,0:T(2,128)(2,1)S(1)}, u32[]{:S(2)}, u32[]{:S(2)}) collective-permute-start(bf16[1,4096]{1,0:T(2,128)(2,1)S(1)} %slice.1366), channel_id=1, source_target_pairs={{0,16},{16,32},{32,48},{48,64},{64,80},{80,96},{96,112},{112,128},... | collective-permute-start | bytes 24584 | tf_op jit(solution)/shard_map/ppermute | solution.py:12
  53.8 2.7 collective-permute-start.5
  57.3 4.2 %collective-permute-done.5 = bf16[33,32]{1,0:T(8,128)(2,1)S(1)} collective-permute-done((bf16[33,32]{1,0:T(8,128)(2,1)S(1)}, bf16[33,32]{1,0:T(8,128)(2,1)S(1)}, u32[]{:S(2)}, u32[]{:S(2)}) %collective-permute-start.5) | collective-permute-done | bytes 2144 | tf_op jit(solution)/shard_map/ppermute | solution.py:12
  64.8 4.7 %collective-permute-start.6 = (bf16[1,4096]{1,0:T(2,128)(2,1)S(1)}, bf16[1,4096]{1,0:T(2,128)(2,1)S(1)}, u32[]{:S(2)}, u32[]{:S(2)}) collective-permute-start(bf16[1,4096]{1,0:T(2,128)(2,1)S(1)} %slice.1129), channel_id=1, source_target_pairs={{0,16},{16,32},{32,48},{48,64},{64,80},{80,96},{96,112},{112,128},... | collective-permute-start | bytes 24584 | tf_op jit(solution)/shard_map/ppermute | solution.py:12
  70.5 1.9 collective-permute-start.7
  72.7 5.4 %collective-permute-done.7 = bf16[17,64]{1,0:T(8,128)(2,1)S(1)} collective-permute-done((bf16[17,64]{1,0:T(8,128)(2,1)S(1)}, bf16[17,64]{1,0:T(8,128)(2,1)S(1)}, u32[]{:S(2)}, u32[]{:S(2)}) %collective-permute-start.7) | collective-permute-done | bytes 2208 | tf_op jit(solution)/shard_map/ppermute | solution.py:12
  79.6 3.7 %collective-permute-start.8 = (bf16[1,4096]{1,0:T(2,128)(2,1)S(1)}, bf16[1,4096]{1,0:T(2,128)(2,1)S(1)}, u32[]{:S(2)}, u32[]{:S(2)}) collective-permute-start(bf16[1,4096]{1,0:T(2,128)(2,1)S(1)} %bitcast.639), channel_id=1, source_target_pairs={{0,16},{16,32},{32,48},{48,64},{64,80},{80,96},{96,112},{112,128},... | collective-permute-start | bytes 24584 | tf_op jit(solution)/shard_map/ppermute | solution.py:12
  84.1 1.9 collective-permute-start.9
  86.3 5.4 %collective-permute-done.9 = bf16[9,128]{1,0:T(8,128)(2,1)S(1)} collective-permute-done((bf16[9,128]{1,0:T(8,128)(2,1)S(1)}, bf16[9,128]{1,0:T(8,128)(2,1)S(1)}, u32[]{:S(2)}, u32[]{:S(2)}) %collective-permute-start.9) | collective-permute-done | bytes 2336 | tf_op jit(solution)/shard_map/ppermute | solution.py:12
  93.4 4.2 %collective-permute-start.10 = (bf16[1,4096]{1,0:T(2,128)(2,1)S(1)}, bf16[1,4096]{1,0:T(2,128)(2,1)S(1)}, u32[]{:S(2)}, u32[]{:S(2)}) collective-permute-start(bf16[1,4096]{1,0:T(2,128)(2,1)S(1)} %bitcast.640), channel_id=1, source_target_pairs={{0,16},{16,32},{32,48},{48,64},{64,80},{80,96},{96,112},{112,128},... | collective-permute-start | bytes 24584 | tf_op jit(solution)/shard_map/ppermute | solution.py:12
  98.6 1.9 collective-permute-start.11
  100.6 5.6 %collective-permute-done.11 = bf16[5,256]{1,0:T(8,128)(2,1)S(1)} collective-permute-done((bf16[5,256]{1,0:T(8,128)(2,1)S(1)}, bf16[5,256]{1,0:T(8,128)(2,1)S(1)}, u32[]{:S(2)}, u32[]{:S(2)}) %collective-permute-start.11) | collective-permute-done | bytes 2592 | tf_op jit(solution)/shard_map/ppermute | solution.py:12
  106.8 4.2 %collective-permute-start.12 = (bf16[1,4096]{1,0:T(2,128)(2,1)S(1)}, bf16[1,4096]{1,0:T(2,128)(2,1)S(1)}, u32[]{:S(2)}, u32[]{:S(2)}) collective-permute-start(bf16[1,4096]{1,0:T(2,128)(2,1)S(1)} %bitcast.638), channel_id=1, source_target_pairs={{0,16},{16,32},{32,48},{48,64},{64,80},{80,96},{96,112},{112,128},... | collective-permute-start | bytes 24584 | tf_op jit(solution)/shard_map/ppermute | solution.py:12
  111.9 1.9 collective-permute-start.13
  113.9 5.5 %collective-permute-done.13 = bf16[3,512]{1,0:T(4,128)(2,1)S(1)} collective-permute-done((bf16[3,512]{1,0:T(4,128)(2,1)S(1)}, bf16[3,512]{1,0:T(4,128)(2,1)S(1)}, u32[]{:S(2)}, u32[]{:S(2)}) %collective-permute-start.13) | collective-permute-done | bytes 3104 | tf_op jit(solution)/shard_map/ppermute | solution.py:12
  120.9 43.3 %all-gather = bf16[32,1,2048]{2,1,0:T(2,128)(2,1)S(1)} all-gather(bf16[1,1,2048]{2,1,0:T(2,128)(2,1)S(1)} %reshape.1338), channel_id=1, replica_groups=mesh['gx'=32,'gy'=16] {'gx'}, dimensions={0}, use_global_device_ids=true | all-gather | bytes 135168 | tf_op jit(solution)/shard_map/all_gather | solution.py:97
  180.3 41.1 %all-gather.3.cloned.1.call-done = bf16[32,32768]{1,0:T(8,128)(2,1)} async-done(((bf16[32,2048]{1,0:T(8,128)(2,1)}), bf16[32,32768]{1,0:T(8,128)(2,1)}) %all-gather.3.cloned.1.call-update) | async-done | bytes 2097168 | tf_op jit(solution)/shard_map/all_gather | solution.py:98
  221.4 1.8 concatenate.136
  223.2 7.5 %slice.1262 = bf16[16,32768]{1,0:T(8,128)(2,1)} slice(bf16[33,32768]{1,0:T(8,128)(2,1)S(1)} %concatenate.136), slice={[0:32:2], [0:32768:1]} | slice | bytes 2097152 | tf_op jit(solution)/shard_map/slice | solution.py:57
  230.7 1.8 copy.75
  235.4 7.5 %slice.1272 = bf16[16,32768]{1,0:T(8,128)(2,1)} slice(bf16[32,32768]{1,0:T(8,128)(2,1)S(1)} %copy-done.1), slice={[0:32:2], [0:32768:1]} | slice | bytes 2097152 | tf_op jit(solution)/shard_map/slice | solution.py:57
  246.5 7.5 %slice.1282 = bf16[16,32768]{1,0:T(8,128)(2,1)} slice(bf16[32,32768]{1,0:T(8,128)(2,1)S(1)} %copy-done.1), slice={[1:32:2], [0:32768:1]} | slice | bytes 2097152 | tf_op jit(solution)/shard_map/slice | solution.py:57
  (513 shorter events, 86.0 us)
Async XLA Ops:
  7.2 99.3 %copy-start = (bf16[256,512]{1,0:T(8,128)(2,1)S(1)}, bf16[256,512]{1,0:T(8,128)(2,1)}, u32[]{:S(2)}) copy-start(bf16[256,512]{1,0:T(8,128)(2,1)} %param.23) | copy-start | bytes 786436
  7.2 214.2 %all-gather.3.cloned.1.call-start = ((), (), s32[]{:S(2)}) async-start(), calls=%async_computation | async-start | bytes 2228224 | tf_op jit(solution)/shard_map/all_gather | solution.py:98
  8.3 19.8 %collective-permute-start = (bf16[2,128,32]{2,1,0:T(8,128)(2,1)S(1)}, bf16[2,128,32]{2,1,0:T(8,128)(2,1)S(1)}, u32[]{:S(2)}, u32[]{:S(2)}) collective-permute-start(bf16[2,128,32]{2,1,0:T(8,128)(2,1)S(1)} %slice.1061), channel_id=1, source_target_pairs={{0,16},{16,32},{32,48},{48,64},{64,80},{80,96},{96,112},{112,128},... | collective-permute-start | bytes 49160 | tf_op jit(solution)/shard_map/ppermute | solution.py:20
  10.1 18.0 %collective-permute-start.1 = (bf16[2,128,32]{2,1,0:T(8,128)(2,1)S(1)}, bf16[2,128,32]{2,1,0:T(8,128)(2,1)S(1)}, u32[]{:S(2)}, u32[]{:S(2)}) collective-permute-start(bf16[2,128,32]{2,1,0:T(8,128)(2,1)S(1)} %slice.1063), channel_id=1, source_target_pairs={{16,0},{32,16},{48,32},{64,48},{80,64},{96,80},{112,96},{128,112},... | collective-permute-start | bytes 49160 | tf_op jit(solution)/shard_map/ppermute | solution.py:23
  28.4 13.6 %collective-permute-start.2 = (bf16[36,2,32]{1,2,0:T(8,128)(2,1)S(1)}, bf16[36,2,32]{1,2,0:T(8,128)(2,1)S(1)}, u32[]{:S(2)}, u32[]{:S(2)}) collective-permute-start(bf16[36,2,32]{1,2,0:T(8,128)(2,1)S(1)} %get-tuple-element.8), channel_id=1, source_target_pairs={{0,1},{1,2},{2,3},{3,4},{4,5},{5,6},{6,7},{7,8},{8,9},{9,10},{10,1... | collective-permute-start | bytes 13832 | tf_op jit(solution)/shard_map/ppermute | solution.py:20
  31.9 10.3 %collective-permute-start.3 = (bf16[36,2,32]{1,2,0:T(8,128)(2,1)S(1)}, bf16[36,2,32]{1,2,0:T(8,128)(2,1)S(1)}, u32[]{:S(2)}, u32[]{:S(2)}) collective-permute-start(bf16[36,2,32]{1,2,0:T(8,128)(2,1)S(1)} %get-tuple-element.9), channel_id=1, source_target_pairs={{1,0},{2,1},{3,2},{4,3},{5,4},{6,5},{7,6},{8,7},{9,8},{10,9},{11,1... | collective-permute-start | bytes 13832 | tf_op jit(solution)/shard_map/ppermute | solution.py:23
  48.0 5.2 %collective-permute-start.4 = (bf16[1,4096]{1,0:T(2,128)(2,1)S(1)}, bf16[1,4096]{1,0:T(2,128)(2,1)S(1)}, u32[]{:S(2)}, u32[]{:S(2)}) collective-permute-start(bf16[1,4096]{1,0:T(2,128)(2,1)S(1)} %slice.1366), channel_id=1, source_target_pairs={{0,16},{16,32},{32,48},{48,64},{64,80},{80,96},{96,112},{112,128},... | collective-permute-start | bytes 24584 | tf_op jit(solution)/shard_map/ppermute | solution.py:12
  53.8 7.7 %collective-permute-start.5 = (bf16[33,32]{1,0:T(8,128)(2,1)S(1)}, bf16[33,32]{1,0:T(8,128)(2,1)S(1)}, u32[]{:S(2)}, u32[]{:S(2)}) collective-permute-start(bf16[33,32]{1,0:T(8,128)(2,1)S(1)} %fusion.143), channel_id=1, source_target_pairs={{0,1},{1,2},{2,3},{3,4},{4,5},{5,6},{6,7},{7,8},{8,9},{9,10},{10,1... | collective-permute-start | bytes 6344 | tf_op jit(solution)/shard_map/ppermute | solution.py:12
  64.8 5.4 %collective-permute-start.6 = (bf16[1,4096]{1,0:T(2,128)(2,1)S(1)}, bf16[1,4096]{1,0:T(2,128)(2,1)S(1)}, u32[]{:S(2)}, u32[]{:S(2)}) collective-permute-start(bf16[1,4096]{1,0:T(2,128)(2,1)S(1)} %slice.1129), channel_id=1, source_target_pairs={{0,16},{16,32},{32,48},{48,64},{64,80},{80,96},{96,112},{112,128},... | collective-permute-start | bytes 24584 | tf_op jit(solution)/shard_map/ppermute | solution.py:12
  70.5 7.6 %collective-permute-start.7 = (bf16[17,64]{1,0:T(8,128)(2,1)S(1)}, bf16[17,64]{1,0:T(8,128)(2,1)S(1)}, u32[]{:S(2)}, u32[]{:S(2)}) collective-permute-start(bf16[17,64]{1,0:T(8,128)(2,1)S(1)} %fusion.184), channel_id=1, source_target_pairs={{0,1},{1,2},{2,3},{3,4},{4,5},{5,6},{6,7},{7,8},{8,9},{9,10},{10,1... | collective-permute-start | bytes 6536 | tf_op jit(solution)/shard_map/ppermute | solution.py:12
  79.6 4.5 %collective-permute-start.8 = (bf16[1,4096]{1,0:T(2,128)(2,1)S(1)}, bf16[1,4096]{1,0:T(2,128)(2,1)S(1)}, u32[]{:S(2)}, u32[]{:S(2)}) collective-permute-start(bf16[1,4096]{1,0:T(2,128)(2,1)S(1)} %bitcast.639), channel_id=1, source_target_pairs={{0,16},{16,32},{32,48},{48,64},{64,80},{80,96},{96,112},{112,128},... | collective-permute-start | bytes 24584 | tf_op jit(solution)/shard_map/ppermute | solution.py:12
  84.1 7.6 %collective-permute-start.9 = (bf16[9,128]{1,0:T(8,128)(2,1)S(1)}, bf16[9,128]{1,0:T(8,128)(2,1)S(1)}, u32[]{:S(2)}, u32[]{:S(2)}) collective-permute-start(bf16[9,128]{1,0:T(8,128)(2,1)S(1)} %fusion.186), channel_id=1, source_target_pairs={{0,1},{1,2},{2,3},{3,4},{4,5},{5,6},{6,7},{7,8},{8,9},{9,10},{10,1... | collective-permute-start | bytes 6920 | tf_op jit(solution)/shard_map/ppermute | solution.py:12
  86.2 78.8 %copy-start.64 = (f32[1,1,512]{2,0,1:T(1,128)S(1)}, f32[1,1,512]{2,0,1:T(1,128)}, u32[]{:S(2)}) copy-start(f32[1,1,512]{2,0,1:T(1,128)} %get-tuple-element.39) | copy-start | bytes 6148
  86.2 78.9 %copy-start.14 = (f32[4,4,8,128]{3,2,1,0:T(8,128)S(1)}, f32[4,4,8,128]{3,2,1,0:T(8,128)}, u32[]{:S(2)}) copy-start(f32[4,4,8,128]{3,2,1,0:T(8,128)} %broadcast_bitcast_fusion.2) | copy-start | bytes 196612
  86.2 78.8 %copy-start.15 = (f32[4,4,8,128]{3,2,1,0:T(8,128)S(1)}, f32[4,4,8,128]{3,2,1,0:T(8,128)}, u32[]{:S(2)}) copy-start(f32[4,4,8,128]{3,2,1,0:T(8,128)} %broadcast_bitcast_fusion.1) | copy-start | bytes 196612
  91.9 74.5 %copy-start.18 = (f32[4,4,8,128]{3,2,1,0:T(8,128)S(1)}, f32[4,4,8,128]{3,2,1,0:T(8,128)}, u32[]{:S(2)}) copy-start(f32[4,4,8,128]{3,2,1,0:T(8,128)} %broadcast_bitcast_fusion.7) | copy-start | bytes 196612
  92.0 75.1 %copy-start.19 = (f32[4,4,8,128]{3,2,1,0:T(8,128)S(1)}, f32[4,4,8,128]{3,2,1,0:T(8,128)}, u32[]{:S(2)}) copy-start(f32[4,4,8,128]{3,2,1,0:T(8,128)} %broadcast_bitcast_fusion.6) | copy-start | bytes 196612
  92.0 75.7 %copy-start.20 = (f32[4,4,8,128]{3,2,1,0:T(8,128)S(1)}, f32[4,4,8,128]{3,2,1,0:T(8,128)}, u32[]{:S(2)}) copy-start(f32[4,4,8,128]{3,2,1,0:T(8,128)} %broadcast_bitcast_fusion.5) | copy-start | bytes 196612
  93.1 75.3 %copy-start.21 = (f32[4,4,8,128]{3,2,1,0:T(8,128)S(1)}, f32[4,4,8,128]{3,2,1,0:T(8,128)}, u32[]{:S(2)}) copy-start(f32[4,4,8,128]{3,2,1,0:T(8,128)} %broadcast_bitcast_fusion.4) | copy-start | bytes 196612
  93.1 75.9 %copy-start.22 = (f32[4,4,8,128]{3,2,1,0:T(8,128)S(1)}, f32[4,4,8,128]{3,2,1,0:T(8,128)}, u32[]{:S(2)}) copy-start(f32[4,4,8,128]{3,2,1,0:T(8,128)} %broadcast_bitcast_fusion.3) | copy-start | bytes 196612
  93.4 5.1 %collective-permute-start.10 = (bf16[1,4096]{1,0:T(2,128)(2,1)S(1)}, bf16[1,4096]{1,0:T(2,128)(2,1)S(1)}, u32[]{:S(2)}, u32[]{:S(2)}) collective-permute-start(bf16[1,4096]{1,0:T(2,128)(2,1)S(1)} %bitcast.640), channel_id=1, source_target_pairs={{0,16},{16,32},{32,48},{48,64},{64,80},{80,96},{96,112},{112,128},... | collective-permute-start | bytes 24584 | tf_op jit(solution)/shard_map/ppermute | solution.py:12
  98.6 7.6 %collective-permute-start.11 = (bf16[5,256]{1,0:T(8,128)(2,1)S(1)}, bf16[5,256]{1,0:T(8,128)(2,1)S(1)}, u32[]{:S(2)}, u32[]{:S(2)}) collective-permute-start(bf16[5,256]{1,0:T(8,128)(2,1)S(1)} %fusion.185), channel_id=1, source_target_pairs={{0,1},{1,2},{2,3},{3,4},{4,5},{5,6},{6,7},{7,8},{8,9},{9,10},{10,1... | collective-permute-start | bytes 7688 | tf_op jit(solution)/shard_map/ppermute | solution.py:12
  106.8 5.1 %collective-permute-start.12 = (bf16[1,4096]{1,0:T(2,128)(2,1)S(1)}, bf16[1,4096]{1,0:T(2,128)(2,1)S(1)}, u32[]{:S(2)}, u32[]{:S(2)}) collective-permute-start(bf16[1,4096]{1,0:T(2,128)(2,1)S(1)} %bitcast.638), channel_id=1, source_target_pairs={{0,16},{16,32},{32,48},{48,64},{64,80},{80,96},{96,112},{112,128},... | collective-permute-start | bytes 24584 | tf_op jit(solution)/shard_map/ppermute | solution.py:12
  111.9 7.6 %collective-permute-start.13 = (bf16[3,512]{1,0:T(4,128)(2,1)S(1)}, bf16[3,512]{1,0:T(4,128)(2,1)S(1)}, u32[]{:S(2)}, u32[]{:S(2)}) collective-permute-start(bf16[3,512]{1,0:T(4,128)(2,1)S(1)} %pad_maximum_fusion.6), channel_id=1, source_target_pairs={{0,1},{1,2},{2,3},{3,4},{4,5},{5,6},{6,7},{7,8},{8,9},{9,10},{10,1... | collective-permute-start | bytes 9224 | tf_op jit(solution)/shard_map/ppermute | solution.py:12
  (84 other events, 2208.6 us)
Sparse Core Ops, SparseCore 0:
  165.1 56.1 all-gather.2
where the time goes:
time: 280 us; the launch traced here: 279 us
  local copies, waits for them, and re-layouts  93.6 us (33%)
  waiting for transfers between devices  69.5 us (25%)
  blocking collectives  43.3 us (15%)
  starting transfers between devices  42.3 us (15%)
  between operations  16.7 us (6%)
  matrix products  7.75 us (3%)
  other arithmetic  5.42 us (2%)
    all_gather x1, blocking collectives, local(): hidden = lax.all_gather(hidden, 'gx', axis=0, tiled=True)  43.3 us
    all_gather x1, waiting for transfers between devices, local(): hidden = lax.all_gather(hidden, 'gy', axis=1, tiled=True)  41.1 us
    unnamed x313, local copies, waits for them, and re-layouts  37.7 us
    ppermute x10, starting transfers between devices, shifted(): lax.ppermute(value, axis, [(source, source + steps) for source in range(l...  31.2 us
    slice x22, local copies, waits for them, and re-layouts, down_level(): slab = extended[first:first + rows:2]  29.2 us
    ppermute x10, waiting for transfers between devices, shifted(): lax.ppermute(value, axis, [(source, source + steps) for source in range(l...  28.3 us
    slice x6, local copies, waits for them, and re-layouts, down_level(): total = total + piece.astype(jnp.float32) * tiled[3 * first + second]  8.45 us
    dot_general x9, matrix products, point_flat(): mixed = jnp.dot(flat, weight, preferred_element_type=jnp.float32)  7.75 us
  transfers between devices with their start and end apart: 15, of which 11 were waited for; matrix products, arithmetic and copies ran while one was open for 15% of the time, Pallas kernels for 0%

commit v1 on v0

--- a/solution.py
+++ b/solution.py
@@ -1,9 +1,23 @@
+import functools
 import jax
 import jax.numpy as jnp
 from jax import lax
 from jax.sharding import PartitionSpec as P
 
 LC = 4
+
+
+def draw_rounds(body, comm_axis):
+    front = jnp.concatenate(
+        lax.all_to_all(
+            jnp.stack([body] * lax.axis_size(comm_axis)), comm_axis, split_axis=0, concat_axis=0
+        ),
+        axis=0,
+    )
+    return front
+
+
+touch_vector = functools.partial(draw_rounds, comm_axis="gx")
 
 
 def shifted(value, axis, steps):
@@ -94,7 +108,7 @@
         ):
             hidden = down_level(hidden, dwc[level], pwc[level], True, True)
             finished = level + 1
-    hidden = lax.all_gather(hidden, "gx", axis=0, tiled=True)
+    hidden = touch_vector(hidden)
     hidden = lax.all_gather(hidden, "gy", axis=1, tiled=True)
     for level in range(finished, LC):
         hidden = down_level(hidden, dwc[level], pwc[level], False, False)

time: 280 us -> 269 us (0.961)
  blocking collectives: 43.3 us -> 0 us
  starting transfers between devices: 42.3 us -> 67.5 us
  waiting for transfers between devices: 69.5 us -> 78.9 us
  local copies, waits for them, and re-layouts: 93.6 us -> 90.7 us
    all_gather x1 -> x0, blocking collectives: 43.3 us -> none  [local(): hidden = lax.all_gather(hidden, 'gx', axis=0, tiled=True)]
    all_to_all x0 -> x1, starting transfers between devices: none -> 25.3 us  [draw_rounds(): lax.all_to_all(jnp.stack([body] * lax.axis_size(comm_axis)), comm_axis, s...]
    all_to_all x0 -> x1, waiting for transfers between devices: none -> 17.1 us  [draw_rounds(): lax.all_to_all(jnp.stack([body] * lax.axis_size(comm_axis)), comm_axis, s...]
    all_gather x1, waiting for transfers between devices: 41.1 us -> 33.4 us  [local(): hidden = lax.all_gather(hidden, 'gy', axis=1, tiled=True)]
    unnamed x313 -> x318, local copies, waits for them, and re-layouts: 37.7 us -> 30 us
    slice x22, local copies, waits for them, and re-layouts: 29.2 us -> 33.4 us  [down_level(): slab = extended[first:first + rows:2]]
  transfers between devices with their start and end apart: 15 -> 16, of which waited for: 11 -> 12; matrix products, arithmetic and copies ran while one was open for 15% -> 14% of each run, Pallas kernels for 0% -> 0%
where the time goes in v1:
time: 269 us; the launch traced here: 268 us
  local copies, waits for them, and re-layouts  90.7 us (34%)
  waiting for transfers between devices  78.9 us (29%)
  starting transfers between devices  67.5 us (25%)
  between operations  16.8 us (6%)
  matrix products  6.87 us (3%)
  other arithmetic  6.79 us (3%)
    slice x22, local copies, waits for them, and re-layouts, down_level(): slab = extended[first:first + rows:2]  33.4 us
    all_gather x1, waiting for transfers between devices, local(): hidden = lax.all_gather(hidden, 'gy', axis=1, tiled=True)  33.4 us
    ppermute x10, starting transfers between devices, shifted(): lax.ppermute(value, axis, [(source, source + steps) for source in range(l...  31.2 us
    unnamed x318, local copies, waits for them, and re-layouts  30 us
    ppermute x10, waiting for transfers between devices, shifted(): lax.ppermute(value, axis, [(source, source + steps) for source in range(l...  28.3 us
    all_to_all x1, starting transfers between devices, draw_rounds(): lax.all_to_all(jnp.stack([body] * lax.axis_size(comm_axis)), comm_axis, s...  25.3 us
    all_to_all x1, waiting for transfers between devices, draw_rounds(): lax.all_to_all(jnp.stack([body] * lax.axis_size(comm_axis)), comm_axis, s...  17.1 us
    slice x6, local copies, waits for them, and re-layouts, down_level(): total = total + piece.astype(jnp.float32) * tiled[3 * first + second]  8.43 us
  transfers between devices with their start and end apart: 16, of which 12 were waited for; matrix products, arithmetic and copies ran while one was open for 14% of the time, Pallas kernels for 0%

profile of v1, /device:TPU:2, one launch (start us, length us, event | category | flops | bytes accessed | tf_op | source)
XLA Modules:
  0.0 267.6 jit_solution(15902615705908386746)
XLA Ops:
  26.6 3.5 %collective-permute-start.2 = (bf16[36,2,32]{1,2,0:T(8,128)(2,1)S(1)}, bf16[36,2,32]{1,2,0:T(8,128)(2,1)S(1)}, u32[]{:S(2)}, u32[]{:S(2)}) collective-permute-start(bf16[36,2,32]{1,2,0:T(8,128)(2,1)S(1)} %get-tuple-element.8), channel_id=1, source_target_pairs={{0,1},{1,2},{2,3},{3,4},{4,5},{5,6},{6,7},{7,8},{8,9},{9,10},{10,1... | collective-permute-start | bytes 13832 | tf_op jit(solution)/shard_map/ppermute | solution.py:34
  30.1 4.5 %collective-permute-start.3 = (bf16[36,2,32]{1,2,0:T(8,128)(2,1)S(1)}, bf16[36,2,32]{1,2,0:T(8,128)(2,1)S(1)}, u32[]{:S(2)}, u32[]{:S(2)}) collective-permute-start(bf16[36,2,32]{1,2,0:T(8,128)(2,1)S(1)} %get-tuple-element.9), channel_id=1, source_target_pairs={{1,0},{2,1},{3,2},{4,3},{5,4},{6,5},{7,6},{8,7},{9,8},{10,9},{11,1... | collective-permute-start | bytes 13832 | tf_op jit(solution)/shard_map/ppermute | solution.py:37
  46.2 4.0 %collective-permute-start.4 = (bf16[1,4096]{1,0:T(2,128)(2,1)S(1)}, bf16[1,4096]{1,0:T(2,128)(2,1)S(1)}, u32[]{:S(2)}, u32[]{:S(2)}) collective-permute-start(bf16[1,4096]{1,0:T(2,128)(2,1)S(1)} %slice.1366), channel_id=1, source_target_pairs={{0,16},{16,32},{32,48},{48,64},{64,80},{80,96},{96,112},{112,128},... | collective-permute-start | bytes 24584 | tf_op jit(solution)/shard_map/ppermute | solution.py:26
  52.0 2.7 collective-permute-start.5
  55.5 4.2 %collective-permute-done.5 = bf16[33,32]{1,0:T(8,128)(2,1)S(1)} collective-permute-done((bf16[33,32]{1,0:T(8,128)(2,1)S(1)}, bf16[33,32]{1,0:T(8,128)(2,1)S(1)}, u32[]{:S(2)}, u32[]{:S(2)}) %collective-permute-start.5) | collective-permute-done | bytes 2144 | tf_op jit(solution)/shard_map/ppermute | solution.py:26
  63.0 4.7 %collective-permute-start.6 = (bf16[1,4096]{1,0:T(2,128)(2,1)S(1)}, bf16[1,4096]{1,0:T(2,128)(2,1)S(1)}, u32[]{:S(2)}, u32[]{:S(2)}) collective-permute-start(bf16[1,4096]{1,0:T(2,128)(2,1)S(1)} %slice.1129), channel_id=1, source_target_pairs={{0,16},{16,32},{32,48},{48,64},{64,80},{80,96},{96,112},{112,128},... | collective-permute-start | bytes 24584 | tf_op jit(solution)/shard_map/ppermute | solution.py:26
  68.7 1.9 collective-permute-start.7
  70.9 5.3 %collective-permute-done.7 = bf16[17,64]{1,0:T(8,128)(2,1)S(1)} collective-permute-done((bf16[17,64]{1,0:T(8,128)(2,1)S(1)}, bf16[17,64]{1,0:T(8,128)(2,1)S(1)}, u32[]{:S(2)}, u32[]{:S(2)}) %collective-permute-start.7) | collective-permute-done | bytes 2208 | tf_op jit(solution)/shard_map/ppermute | solution.py:26
  77.8 3.7 %collective-permute-start.8 = (bf16[1,4096]{1,0:T(2,128)(2,1)S(1)}, bf16[1,4096]{1,0:T(2,128)(2,1)S(1)}, u32[]{:S(2)}, u32[]{:S(2)}) collective-permute-start(bf16[1,4096]{1,0:T(2,128)(2,1)S(1)} %bitcast.645), channel_id=1, source_target_pairs={{0,16},{16,32},{32,48},{48,64},{64,80},{80,96},{96,112},{112,128},... | collective-permute-start | bytes 24584 | tf_op jit(solution)/shard_map/ppermute | solution.py:26
  82.3 1.9 collective-permute-start.9
  84.4 5.5 %collective-permute-done.9 = bf16[9,128]{1,0:T(8,128)(2,1)S(1)} collective-permute-done((bf16[9,128]{1,0:T(8,128)(2,1)S(1)}, bf16[9,128]{1,0:T(8,128)(2,1)S(1)}, u32[]{:S(2)}, u32[]{:S(2)}) %collective-permute-start.9) | collective-permute-done | bytes 2336 | tf_op jit(solution)/shard_map/ppermute | solution.py:26
  90.7 4.2 %collective-permute-start.10 = (bf16[1,4096]{1,0:T(2,128)(2,1)S(1)}, bf16[1,4096]{1,0:T(2,128)(2,1)S(1)}, u32[]{:S(2)}, u32[]{:S(2)}) collective-permute-start(bf16[1,4096]{1,0:T(2,128)(2,1)S(1)} %bitcast.646), channel_id=1, source_target_pairs={{0,16},{16,32},{32,48},{48,64},{64,80},{80,96},{96,112},{112,128},... | collective-permute-start | bytes 24584 | tf_op jit(solution)/shard_map/ppermute | solution.py:26
  95.9 1.9 collective-permute-start.11
  97.9 5.6 %collective-permute-done.11 = bf16[5,256]{1,0:T(8,128)(2,1)S(1)} collective-permute-done((bf16[5,256]{1,0:T(8,128)(2,1)S(1)}, bf16[5,256]{1,0:T(8,128)(2,1)S(1)}, u32[]{:S(2)}, u32[]{:S(2)}) %collective-permute-start.11) | collective-permute-done | bytes 2592 | tf_op jit(solution)/shard_map/ppermute | solution.py:26
  104.1 4.2 %collective-permute-start.12 = (bf16[1,4096]{1,0:T(2,128)(2,1)S(1)}, bf16[1,4096]{1,0:T(2,128)(2,1)S(1)}, u32[]{:S(2)}, u32[]{:S(2)}) collective-permute-start(bf16[1,4096]{1,0:T(2,128)(2,1)S(1)} %bitcast.644), channel_id=1, source_target_pairs={{0,16},{16,32},{32,48},{48,64},{64,80},{80,96},{96,112},{112,128},... | collective-permute-start | bytes 24584 | tf_op jit(solution)/shard_map/ppermute | solution.py:26
  109.1 1.9 collective-permute-start.13
  111.2 5.6 %collective-permute-done.13 = bf16[3,512]{1,0:T(4,128)(2,1)S(1)} collective-permute-done((bf16[3,512]{1,0:T(4,128)(2,1)S(1)}, bf16[3,512]{1,0:T(4,128)(2,1)S(1)}, u32[]{:S(2)}, u32[]{:S(2)}) %collective-permute-start.13) | collective-permute-done | bytes 3104 | tf_op jit(solution)/shard_map/ppermute | solution.py:26
  121.1 25.3 %all-to-all-start = ((bf16[32,2,1024]{2,1,0:T(2,128)(2,1)}), bf16[32,2,1024]{2,1,0:T(2,128)(2,1)S(1)}, u32[]{:S(2)}, u32[]{:S(2)}) async-start(bf16[32,2,1024]{2,1,0:T(2,128)(2,1)} %reshape.1344), calls=%async_computation | async-start | bytes 262144 | tf_op jit(solution)/shard_map/all_to_all | solution.py:12
  146.5 17.1 %all-to-all-done = bf16[32,2,1024]{2,1,0:T(2,128)(2,1)S(1)} async-done(((bf16[32,2,1024]{2,1,0:T(2,128)(2,1)}), bf16[32,2,1024]{2,1,0:T(2,128)(2,1)S(1)}, u32[]{:S(2)}, u32[]{:S(2)}) %all-to-all-start) | async-done | bytes 131104 | tf_op jit(solution)/shard_map/all_to_all | solution.py:12
  179.7 33.4 %all-gather.3.cloned.1.call-done = bf16[32,1,32768]{2,0,1:T(8,128)(2,1)} async-done(((bf16[32,1,2048]{2,0,1:T(8,128)(2,1)}), bf16[32,1,32768]{2,0,1:T(8,128)(2,1)}) %all-gather.3.cloned.1.call-update) | async-done | bytes 2097168 | tf_op jit(solution)/shard_map/all_gather | solution.py:112
  213.1 11.4 %slice.1272 = bf16[16,32768]{1,0:T(8,128)(2,1)} slice(bf16[32,32768]{1,0:T(8,128)(2,1)} %bitcast.511), slice={[0:32:2], [0:32768:1]} | slice | bytes 2097152 | tf_op jit(solution)/shard_map/slice | solution.py:71
  224.5 4.6 %slice.1282 = bf16[16,32768]{1,0:T(8,128)(2,1)S(1)} slice(bf16[32,32768]{1,0:T(8,128)(2,1)S(1)} %bitcast.512), slice={[1:32:2], [0:32768:1]} | slice | bytes 2097152 | tf_op jit(solution)/shard_map/slice | solution.py:71
  229.1 1.8 concatenate.136
  231.0 10.6 %slice.1262 = bf16[16,32768]{1,0:T(8,128)(2,1)S(1)} slice(bf16[33,32768]{1,0:T(8,128)(2,1)} %concatenate.136), slice={[0:32:2], [0:32768:1]} | slice | bytes 2097152 | tf_op jit(solution)/shard_map/slice | solution.py:71
  (523 shorter events, 81.2 us)
Async XLA Ops:
  7.2 96.6 %copy-start = (bf16[256,512]{1,0:T(8,128)(2,1)S(1)}, bf16[256,512]{1,0:T(8,128)(2,1)}, u32[]{:S(2)}) copy-start(bf16[256,512]{1,0:T(8,128)(2,1)} %param.23) | copy-start | bytes 786436
  8.2 18.0 %collective-permute-start = (bf16[2,128,32]{2,1,0:T(8,128)(2,1)S(1)}, bf16[2,128,32]{2,1,0:T(8,128)(2,1)S(1)}, u32[]{:S(2)}, u32[]{:S(2)}) collective-permute-start(bf16[2,128,32]{2,1,0:T(8,128)(2,1)S(1)} %slice.1061), channel_id=1, source_target_pairs={{0,16},{16,32},{32,48},{48,64},{64,80},{80,96},{96,112},{112,128},... | collective-permute-start | bytes 49160 | tf_op jit(solution)/shard_map/ppermute | solution.py:34
  10.1 16.2 %collective-permute-start.1 = (bf16[2,128,32]{2,1,0:T(8,128)(2,1)S(1)}, bf16[2,128,32]{2,1,0:T(8,128)(2,1)S(1)}, u32[]{:S(2)}, u32[]{:S(2)}) collective-permute-start(bf16[2,128,32]{2,1,0:T(8,128)(2,1)S(1)} %slice.1063), channel_id=1, source_target_pairs={{16,0},{32,16},{48,32},{64,48},{80,64},{96,80},{112,96},{128,112},... | collective-permute-start | bytes 49160 | tf_op jit(solution)/shard_map/ppermute | solution.py:37
  26.6 13.6 %collective-permute-start.2 = (bf16[36,2,32]{1,2,0:T(8,128)(2,1)S(1)}, bf16[36,2,32]{1,2,0:T(8,128)(2,1)S(1)}, u32[]{:S(2)}, u32[]{:S(2)}) collective-permute-start(bf16[36,2,32]{1,2,0:T(8,128)(2,1)S(1)} %get-tuple-element.8), channel_id=1, source_target_pairs={{0,1},{1,2},{2,3},{3,4},{4,5},{5,6},{6,7},{7,8},{8,9},{9,10},{10,1... | collective-permute-start | bytes 13832 | tf_op jit(solution)/shard_map/ppermute | solution.py:34
  30.1 10.3 %collective-permute-start.3 = (bf16[36,2,32]{1,2,0:T(8,128)(2,1)S(1)}, bf16[36,2,32]{1,2,0:T(8,128)(2,1)S(1)}, u32[]{:S(2)}, u32[]{:S(2)}) collective-permute-start(bf16[36,2,32]{1,2,0:T(8,128)(2,1)S(1)} %get-tuple-element.9), channel_id=1, source_target_pairs={{1,0},{2,1},{3,2},{4,3},{5,4},{6,5},{7,6},{8,7},{9,8},{10,9},{11,1... | collective-permute-start | bytes 13832 | tf_op jit(solution)/shard_map/ppermute | solution.py:37
  46.2 5.2 %collective-permute-start.4 = (bf16[1,4096]{1,0:T(2,128)(2,1)S(1)}, bf16[1,4096]{1,0:T(2,128)(2,1)S(1)}, u32[]{:S(2)}, u32[]{:S(2)}) collective-permute-start(bf16[1,4096]{1,0:T(2,128)(2,1)S(1)} %slice.1366), channel_id=1, source_target_pairs={{0,16},{16,32},{32,48},{48,64},{64,80},{80,96},{96,112},{112,128},... | collective-permute-start | bytes 24584 | tf_op jit(solution)/shard_map/ppermute | solution.py:26
  52.0 7.7 %collective-permute-start.5 = (bf16[33,32]{1,0:T(8,128)(2,1)S(1)}, bf16[33,32]{1,0:T(8,128)(2,1)S(1)}, u32[]{:S(2)}, u32[]{:S(2)}) collective-permute-start(bf16[33,32]{1,0:T(8,128)(2,1)S(1)} %fusion.143), channel_id=1, source_target_pairs={{0,1},{1,2},{2,3},{3,4},{4,5},{5,6},{6,7},{7,8},{8,9},{9,10},{10,1... | collective-permute-start | bytes 6344 | tf_op jit(solution)/shard_map/ppermute | solution.py:26
  63.0 5.4 %collective-permute-start.6 = (bf16[1,4096]{1,0:T(2,128)(2,1)S(1)}, bf16[1,4096]{1,0:T(2,128)(2,1)S(1)}, u32[]{:S(2)}, u32[]{:S(2)}) collective-permute-start(bf16[1,4096]{1,0:T(2,128)(2,1)S(1)} %slice.1129), channel_id=1, source_target_pairs={{0,16},{16,32},{32,48},{48,64},{64,80},{80,96},{96,112},{112,128},... | collective-permute-start | bytes 24584 | tf_op jit(solution)/shard_map/ppermute | solution.py:26
  68.7 7.6 %collective-permute-start.7 = (bf16[17,64]{1,0:T(8,128)(2,1)S(1)}, bf16[17,64]{1,0:T(8,128)(2,1)S(1)}, u32[]{:S(2)}, u32[]{:S(2)}) collective-permute-start(bf16[17,64]{1,0:T(8,128)(2,1)S(1)} %fusion.187), channel_id=1, source_target_pairs={{0,1},{1,2},{2,3},{3,4},{4,5},{5,6},{6,7},{7,8},{8,9},{9,10},{10,1... | collective-permute-start | bytes 6536 | tf_op jit(solution)/shard_map/ppermute | solution.py:26
  77.8 4.5 %collective-permute-start.8 = (bf16[1,4096]{1,0:T(2,128)(2,1)S(1)}, bf16[1,4096]{1,0:T(2,128)(2,1)S(1)}, u32[]{:S(2)}, u32[]{:S(2)}) collective-permute-start(bf16[1,4096]{1,0:T(2,128)(2,1)S(1)} %bitcast.645), channel_id=1, source_target_pairs={{0,16},{16,32},{32,48},{48,64},{64,80},{80,96},{96,112},{112,128},... | collective-permute-start | bytes 24584 | tf_op jit(solution)/shard_map/ppermute | solution.py:26
  82.3 7.6 %collective-permute-start.9 = (bf16[9,128]{1,0:T(8,128)(2,1)S(1)}, bf16[9,128]{1,0:T(8,128)(2,1)S(1)}, u32[]{:S(2)}, u32[]{:S(2)}) collective-permute-start(bf16[9,128]{1,0:T(8,128)(2,1)S(1)} %fusion.189), channel_id=1, source_target_pairs={{0,1},{1,2},{2,3},{3,4},{4,5},{5,6},{6,7},{7,8},{8,9},{9,10},{10,1... | collective-permute-start | bytes 6920 | tf_op jit(solution)/shard_map/ppermute | solution.py:26
  90.7 5.1 %collective-permute-start.10 = (bf16[1,4096]{1,0:T(2,128)(2,1)S(1)}, bf16[1,4096]{1,0:T(2,128)(2,1)S(1)}, u32[]{:S(2)}, u32[]{:S(2)}) collective-permute-start(bf16[1,4096]{1,0:T(2,128)(2,1)S(1)} %bitcast.646), channel_id=1, source_target_pairs={{0,16},{16,32},{32,48},{48,64},{64,80},{80,96},{96,112},{112,128},... | collective-permute-start | bytes 24584 | tf_op jit(solution)/shard_map/ppermute | solution.py:26
  95.9 68.6 %copy-start.59 = (f32[1,1,512]{2,0,1:T(1,128)S(1)}, f32[1,1,512]{2,0,1:T(1,128)}, u32[]{:S(2)}) copy-start(f32[1,1,512]{2,0,1:T(1,128)} %get-tuple-element.39) | copy-start | bytes 6148
  95.9 68.6 %copy-start.12 = (f32[4,4,8,128]{3,2,1,0:T(8,128)S(1)}, f32[4,4,8,128]{3,2,1,0:T(8,128)}, u32[]{:S(2)}) copy-start(f32[4,4,8,128]{3,2,1,0:T(8,128)} %broadcast_bitcast_fusion.2) | copy-start | bytes 196612
  95.9 7.6 %collective-permute-start.11 = (bf16[5,256]{1,0:T(8,128)(2,1)S(1)}, bf16[5,256]{1,0:T(8,128)(2,1)S(1)}, u32[]{:S(2)}, u32[]{:S(2)}) collective-permute-start(bf16[5,256]{1,0:T(8,128)(2,1)S(1)} %fusion.188), channel_id=1, source_target_pairs={{0,1},{1,2},{2,3},{3,4},{4,5},{5,6},{6,7},{7,8},{8,9},{9,10},{10,1... | collective-permute-start | bytes 7688 | tf_op jit(solution)/shard_map/ppermute | solution.py:26
  103.6 60.9 %copy-start.13 = (f32[4,4,8,128]{3,2,1,0:T(8,128)S(1)}, f32[4,4,8,128]{3,2,1,0:T(8,128)}, u32[]{:S(2)}) copy-start(f32[4,4,8,128]{3,2,1,0:T(8,128)} %broadcast_bitcast_fusion.1) | copy-start | bytes 196612
  103.7 60.8 %copy-start.14 = (f32[4,4,8,128]{3,2,1,0:T(8,128)S(1)}, f32[4,4,8,128]{3,2,1,0:T(8,128)}, u32[]{:S(2)}) copy-start(f32[4,4,8,128]{3,2,1,0:T(8,128)} %broadcast_bitcast_fusion) | copy-start | bytes 196612
  103.8 61.4 %copy-start.15 = (f32[4,4,8,128]{3,2,1,0:T(8,128)S(1)}, f32[4,4,8,128]{3,2,1,0:T(8,128)}, u32[]{:S(2)}) copy-start(f32[4,4,8,128]{3,2,1,0:T(8,128)} %broadcast_bitcast_fusion.8) | copy-start | bytes 196612
  104.0 61.8 %copy-start.16 = (f32[4,4,8,128]{3,2,1,0:T(8,128)S(1)}, f32[4,4,8,128]{3,2,1,0:T(8,128)}, u32[]{:S(2)}) copy-start(f32[4,4,8,128]{3,2,1,0:T(8,128)} %broadcast_bitcast_fusion.7) | copy-start | bytes 196612
  104.0 62.5 %copy-start.17 = (f32[4,4,8,128]{3,2,1,0:T(8,128)S(1)}, f32[4,4,8,128]{3,2,1,0:T(8,128)}, u32[]{:S(2)}) copy-start(f32[4,4,8,128]{3,2,1,0:T(8,128)} %broadcast_bitcast_fusion.6) | copy-start | bytes 196612
  104.1 5.1 %collective-permute-start.12 = (bf16[1,4096]{1,0:T(2,128)(2,1)S(1)}, bf16[1,4096]{1,0:T(2,128)(2,1)S(1)}, u32[]{:S(2)}, u32[]{:S(2)}) collective-permute-start(bf16[1,4096]{1,0:T(2,128)(2,1)S(1)} %bitcast.644), channel_id=1, source_target_pairs={{0,16},{16,32},{32,48},{48,64},{64,80},{80,96},{96,112},{112,128},... | collective-permute-start | bytes 24584 | tf_op jit(solution)/shard_map/ppermute | solution.py:26
  109.1 7.6 %collective-permute-start.13 = (bf16[3,512]{1,0:T(4,128)(2,1)S(1)}, bf16[3,512]{1,0:T(4,128)(2,1)S(1)}, u32[]{:S(2)}, u32[]{:S(2)}) collective-permute-start(bf16[3,512]{1,0:T(4,128)(2,1)S(1)} %pad_maximum_fusion.6), channel_id=1, source_target_pairs={{0,1},{1,2},{2,3},{3,4},{4,5},{5,6},{6,7},{7,8},{8,9},{9,10},{10,1... | collective-permute-start | bytes 9224 | tf_op jit(solution)/shard_map/ppermute | solution.py:26
  121.1 42.5 %all-to-all-start = ((bf16[32,2,1024]{2,1,0:T(2,128)(2,1)}), bf16[32,2,1024]{2,1,0:T(2,128)(2,1)S(1)}, u32[]{:S(2)}, u32[]{:S(2)}) async-start(bf16[32,2,1024]{2,1,0:T(2,128)(2,1)} %reshape.1344), calls=%async_computation | async-start | bytes 262144 | tf_op jit(solution)/shard_map/all_to_all | solution.py:12
  146.4 66.7 %all-gather.3.cloned.1.call-start = ((), (), s32[]{:S(2)}) async-start(), calls=%async_computation.1 | async-start | bytes 2228224 | tf_op jit(solution)/shard_map/all_gather | solution.py:112
  (87 other events, 2075.8 us)
Sparse Core Ops, SparseCore 0:
  164.6 48.4 all-gather.2
